TPU v7x, 128 devices: a whole 4x4x4 slice. The times are simulated.
128 devices in a mesh: tok: 32 (over z, x, core), head: 4 (over y).
Axes of the slice: x: 4, y: 4, z: 4, core: 2. Of those that a mesh axis runs over, the one named last changes fastest.
Arguments:
- hidden_in: bfloat16 [32, 512, 5120], P('tok', None, 'head')
- norm_gain: float32 [5120], replicated, may hold values from 0.1 to 1.9
- w_query: bfloat16 [5120, 2048], P(None, 'head'), may hold values from -0.078125 to 0.078125
- w_key: bfloat16 [5120, 512], P(None, 'head'), may hold values from -0.15625 to 0.15625
- w_value: bfloat16 [5120, 512], P(None, 'head'), may hold values from -0.078125 to 0.078125
- w_out: bfloat16 [2048, 5120], P(None, 'head'), may hold values from -0.5 to 0.5
- prefix_cache: bfloat16 [64, 2, 128, 512], P('tok', None, None, 'head')
- suffix_len: int32 [32], replicated, may hold values from 1 to 512, 10240 in all
- page_table: int32 [2, 32], replicated, may hold values from 0 to 63, as said below
- request_group: int32 [32], replicated, may hold values from 0 to 1, as said below
Outputs:
- hidden_out: bfloat16 [32, 512, 5120], P('tok', None, 'head')
Inputs may be any that keep to these rules, and one draw needn't show every extreme that they name: `page_table`: every one of the 64 slots appears exactly once; row g lists the slots that hold group g's prefix pages, page by page. `request_group`: exactly half of the 32 requests are in each group.
All inputs are finite; a program needn't handle non-finite values.
Results may differ from a plain program's by a relative error of at most 0.008.
The roundings to bfloat16 on the way count: a program that leaves them out, or rounds other values in their place, can miss the bound.
Values may be sent and summed in bfloat16 or wider, within the bound.
No kernel may reach another device: no remote copies, remote signals or barrier semaphores. Data moves between devices by JAX's collectives and lax.ppermute only.
A program may use at most 128 MiB of HBM per device.

v0:
```python
import math
import jax
import jax.numpy as jnp
from jax import lax
from jax.sharding import PartitionSpec as P

HD = 128
PREFIX = 4096
THETA = 100000000.0
EPS = 1e-05
NEG = -1e30


def rope_angles(positions, size):
    half = size // 2
    ladder = jnp.arange(half, dtype=jnp.float32)
    freq = jnp.exp(ladder * (-2.0 * jnp.log(THETA) / size))
    angle = positions.astype(jnp.float32)[:, None] * freq[None, :]
    return (jnp.cos(angle), jnp.sin(angle))


def rotate(values, cosine, sine):
    half = values.shape[-1] // 2
    first = values[..., :half]
    second = values[..., half:]
    return jnp.concatenate(
        [first * cosine - second * sine, second * cosine + first * sine], axis=-1
    )


def online_block(carry, queries, block_keys, block_values, allowed):
    highest, total, numerator = carry
    scores = lax.dot_general(
        queries, block_keys, (((1,), (1,)), ((), ())), preferred_element_type=jnp.float32
    )
    scores = jnp.where(allowed, scores * queries.shape[1] ** (-0.5), NEG)
    new_high = jnp.maximum(highest, jnp.max(scores, axis=1))
    weights = jnp.where(allowed, jnp.exp(scores - new_high[:, None]), 0.0)
    factor = jnp.exp(highest - new_high)
    total = total * factor + jnp.sum(weights, axis=1)
    numerator = numerator * factor[:, None] + jnp.dot(
        weights.astype(jnp.bfloat16), block_values, preferred_element_type=jnp.float32
    )
    return (new_high, total, numerator)


def fold_keys(carry, queries, all_keys, all_values, allowed):
    count = all_keys.shape[0]
    block = math.gcd(count, 512)
    rounds = count // block
    if rounds == 1:
        return online_block(carry, queries, all_keys, all_values, allowed)
    key_blocks = all_keys.reshape(rounds, block, all_keys.shape[1])
    value_blocks = all_values.reshape(rounds, block, all_values.shape[1])
    mask_blocks = allowed.reshape(allowed.shape[0], rounds, block).transpose(1, 0, 2)

    def advance(state, items):
        return (online_block(state, queries, items[0], items[1], items[2]), None)

    carry, _ = lax.scan(advance, carry, (key_blocks, value_blocks, mask_blocks))
    return carry


def local(
    hidden_in,
    norm_gain,
    w_query,
    w_key,
    w_value,
    w_out,
    prefix_cache,
    suffix_len,
    page_table,
    request_group,
):
    local_len = hidden_in.shape[1]
    whole = lax.all_gather(hidden_in, "head", axis=2, tiled=True)
    flat = whole.reshape(local_len, whole.shape[2]).astype(jnp.float32)
    inverse = lax.rsqrt(jnp.mean(flat * flat, axis=1, keepdims=True) + EPS)
    normed = (flat * inverse * norm_gain[None, :]).astype(jnp.bfloat16)
    head_size = HD
    kv_local = w_key.shape[1] // head_size
    q_local = w_query.shape[1] // head_size
    per_kv = q_local // kv_local
    device = lax.axis_index("tok")
    positions = PREFIX + jnp.arange(local_len, dtype=jnp.int32)
    cosine, sine = rope_angles(positions, head_size)
    cosine = cosine[:, None, :]
    sine = sine[:, None, :]
    query = jnp.dot(normed, w_query, preferred_element_type=jnp.float32).reshape(
        local_len, q_local, head_size
    )
    query = rotate(query, cosine, sine).astype(jnp.bfloat16)
    keys = jnp.dot(normed, w_key, preferred_element_type=jnp.float32).reshape(
        local_len, kv_local, head_size
    )
    keys = rotate(keys, cosine, sine).astype(jnp.bfloat16)
    values = jnp.dot(normed, w_value, preferred_element_type=jnp.float32).astype(jnp.bfloat16)
    values = values.reshape(local_len, kv_local, head_size)
    length = suffix_len[device]
    group = request_group[device]
    own_pages = page_table[group]
    total_rows = per_kv * local_len
    q_rows = [query.transpose(1, 0, 2).reshape(total_rows, head_size)]
    start_state = (
        jnp.full((total_rows,), NEG, jnp.float32),
        jnp.zeros((total_rows,), jnp.float32),
        jnp.zeros((total_rows, head_size), jnp.float32),
    )
    carry = tuple((start_state for k in range(kv_local)))
    piece = lax.all_gather(prefix_cache, "tok", axis=0, tiled=True)
    count = piece.shape[0]
    slots = jnp.arange(count, dtype=jnp.int32)
    member = jnp.any(own_pages[:, None] == slots[None, :], axis=0)
    allowed = jnp.repeat(member, piece.shape[2])[None, :]
    k = 0
    page_keys = piece[:, 0].reshape(count * piece.shape[2], head_size)
    page_values = piece[:, 1].reshape(count * piece.shape[2], head_size)
    updated = [fold_keys(carry[k], q_rows[k], page_keys, page_values, allowed)]
    carry = tuple(updated)
    query_pos = jnp.arange(total_rows, dtype=jnp.int32) % local_len
    key_pos = jnp.arange(local_len, dtype=jnp.int32)
    causal = (key_pos[None, :] <= query_pos[:, None]) & (key_pos[None, :] < length)
    k = 0
    _, total, numerator = fold_keys(carry[k], q_rows[k], keys[:, k, :], values[:, k, :], causal)
    mixed = (numerator / total[:, None]).astype(jnp.bfloat16)
    pieces = (
        mixed.reshape(per_kv, local_len, head_size)
        .transpose(1, 0, 2)
        .reshape(local_len, per_kv * head_size)
    )
    output = jnp.dot(
        lax.all_gather(pieces, "head", axis=1, tiled=True),
        w_out,
        preferred_element_type=jnp.float32,
    )
    live = jnp.arange(local_len, dtype=jnp.int32) < length
    output = jnp.where(live[:, None], output, 0.0).astype(jnp.bfloat16)
    return output.reshape(1, local_len, w_out.shape[1])


def solution(mesh):
    return jax.shard_map(
        local,
        mesh=mesh,
        in_specs=(
            P("tok", None, "head"),
            P(),
            P(None, "head"),
            P(None, "head"),
            P(None, "head"),
            P(None, "head"),
            P("tok", None, None, "head"),
            P(),
            P(),
            P(),
        ),
        out_specs=P("tok", None, "head"),
        check_vma=False,
    )
```

profile of v0, /device:TPU:1, one launch (start us, length us, event | category | flops | bytes accessed | tf_op | source)
XLA Modules:
  0.0 274.4 jit_solution(10157303807104072718)
XLA Ops:
  8.1 1.3 dynamic_slice.21
  13.7 7.8 %copy.24 = bf16[512,5120]{1,0:T(8,128)(2,1)} copy(bf16[512,5120]{0,1:T(8,128)(2,1)} %bitcast.70) | data formatting | bytes 10485760 | tf_op jit(solution)/shard_map/dot_general | solution.py:90
  22.8 46.2 %all-gather.6.cloned.1.call-done = bf16[1,512,5120]{2,1,0:T(8,128)(2,1)} async-done(((bf16[1,512,1280]{2,1,0:T(8,128)(2,1)}), bf16[1,512,5120]{2,1,0:T(8,128)(2,1)}) %all-gather.6.cloned.1.call-update) | async-done | bytes 5242896 | tf_op jit(solution)/shard_map/all_gather | solution.py:77
  69.0 3.7 %fusion.21 = f32[512]{0:T(512)S(1)} fusion(bf16[1,512,5120]{2,1,0:T(8,128)(2,1)} %all-gather.6.cloned.1.call-done), kind=kLoop, calls=%fused_computation.30 | loop fusion | flops 7863808 | bytes 5244928 | tf_op jit(solution)/shard_map/reduce_sum | solution.py:79
  73.0 5.7 %fusion.27 = f32[512,4,128]{0,2,1:T(8,128)S(1)} fusion(bf16[4,128,5120]{2,1,0:T(8,128)(2,1)} %bitcast.71, bf16[1,512,5120]{2,1,0:T(8,128)(2,1)S(1)} %copy-done.1, f32[5120]{0:T(1024)S(1)} %copy-done.2, f32[512]{0:T(512)S(1)} %add_rsqrt_fusion), kind=kOutput, calls=%fused_computation.36 | convolution fusion | flops 2694840320 | bytes 11556864 | tf_op jit(solution)/shard_map/dot_general | solution.py:90
  79.3 4.9 %fusion.46 = f32[512,1,128]{0,2,1:T(8,128)S(1)} fusion(bf16[5120,128]{1,0:T(8,128)(2,1)} %param.15, bf16[1,512,5120]{2,1,0:T(8,128)(2,1)} %all-gather.6.cloned.1.call-done, f32[5120]{0:T(1024)S(1)} %copy-done.2, f32[512]{0:T(512)S(1)} %add_rsqrt_fusion), kind=kOutput, calls=%fused_computation.56 | convolution fusion | flops 681574400 | bytes 6838272 | tf_op jit(solution)/shard_map/dot_general | solution.py:94
  84.7 3.3 %fusion.74 = (f32[2048]{0:T(1024)S(1)}, f32[2048,512]{0,1:T(8,128)}) fusion(bf16[2048,128]{1,0:T(8,128)(2,1)S(1)} %bitcast.68, bf16[512,64]{0,1:T(8,128)(2,1)S(1)} %get-tuple-element.130, bf16[512,64]{0,1:T(8,128)(2,1)S(1)} %get-tuple-element.129, pred[512]{0:T(512)(128)(4,1)S(1)} %iota_compare_fusion.2, s32[2048]{0:T(1024)S(1)} %add_select_fusion), kind=kOutput, calls=%fused_computation.95 | convolution fusion | flops 273938432 | bytes 4866560 | tf_op jit(solution)/shard_map/dot_general | solution.py:33
  88.1 30.4 %all-gather.4.cloned.1.call-done = bf16[64,2,128,128]{3,2,1,0:T(8,128)(2,1)} async-done(((bf16[2,2,128,128]{3,2,1,0:T(8,128)(2,1)}), bf16[64,2,128,128]{3,2,1,0:T(8,128)(2,1)}) %all-gather.4.cloned.1.call-update) | async-done | bytes 4194320 | tf_op jit(solution)/shard_map/all_gather | solution.py:111
  118.5 4.9 %fusion.73 = (bf16[64,1,128,128]{3,2,1,0:T(8,128)(2,1)}, bf16[64,1,128,128]{3,2,1,0:T(8,128)(2,1)}) fusion(bf16[64,2,128,128]{3,2,1,0:T(8,128)(2,1)} %all-gather.4.cloned.1.call-done), kind=kLoop, calls=%fused_computation.94 | loop fusion | bytes 8388608 | tf_op jit(solution)/shard_map/slice | solution.py:118
  123.4 95.6 %while.15 = (s32[]{:T(128)}, f32[2048]{0:T(1024)S(1)}, f32[2048]{0:T(1024)S(1)}, f32[2048,128]{1,0:T(8,128)S(1)}, pred[16,1,512]{2,1,0:T(4,128)(4,1)S(1)}, /*ind...) while((s32[]{:T(128)}, f32[2048]{0:T(1024)S(1)}, ...), condition=%wide.region_5.6_spmd.clone, body=%wide.region_2.5_spmd.clone.sunk | while | flops 551299072 | bytes 15600261 | solution.py:60
  123.4 1.6 fusion.91
  126.4 2.9 %convolution_add_fusion.3 = f32[2048,128]{1,0:T(8,128)S(1)} fusion(f32[512,2048]{1,0:T(8,128)S(1)} %get-tuple-element.189, f32[2048]{0:T(1024)S(1)} %select_maximum_fusion.2, pred[512]{0:T(512)(128)(4,1)S(1)} %dynamic-slice_reduce_fusion.2, f32[2048,128]{1,0:T(8,128)S(1)} %get-tuple-element.205, f32[2048]{0:T(1024)S(1)} %get-tuple-element.191, ...), kind=kOutput, calls=%fused_computation.5.clone.1 | convolution fusion | flops 274464768 | bytes 6439429 | tf_op jit(solution)/shard_map/while/body/eval_jaxpr/dot_general | solution.py:41
  129.4 1.6 fusion.91
  131.0 1.3 fusion.92
  132.3 2.9 %convolution_add_fusion.3 = f32[2048,128]{1,0:T(8,128)S(1)} fusion(f32[512,2048]{1,0:T(8,128)S(1)} %get-tuple-element.189, f32[2048]{0:T(1024)S(1)} %select_maximum_fusion.2, pred[512]{0:T(512)(128)(4,1)S(1)} %dynamic-slice_reduce_fusion.2, f32[2048,128]{1,0:T(8,128)S(1)} %get-tuple-element.205, f32[2048]{0:T(1024)S(1)} %get-tuple-element.191, ...), kind=kOutput, calls=%fused_computation.5.clone.1 | convolution fusion | flops 274464768 | bytes 6439429 | tf_op jit(solution)/shard_map/while/body/eval_jaxpr/dot_general | solution.py:41
  135.3 1.6 fusion.91
  138.3 2.9 %convolution_add_fusion.3 = f32[2048,128]{1,0:T(8,128)S(1)} fusion(f32[512,2048]{1,0:T(8,128)S(1)} %get-tuple-element.189, f32[2048]{0:T(1024)S(1)} %select_maximum_fusion.2, pred[512]{0:T(512)(128)(4,1)S(1)} %dynamic-slice_reduce_fusion.2, f32[2048,128]{1,0:T(8,128)S(1)} %get-tuple-element.205, f32[2048]{0:T(1024)S(1)} %get-tuple-element.191, ...), kind=kOutput, calls=%fused_computation.5.clone.1 | convolution fusion | flops 274464768 | bytes 6439429 | tf_op jit(solution)/shard_map/while/body/eval_jaxpr/dot_general | solution.py:41
  141.3 1.6 fusion.91
  144.3 2.9 %convolution_add_fusion.3 = f32[2048,128]{1,0:T(8,128)S(1)} fusion(f32[512,2048]{1,0:T(8,128)S(1)} %get-tuple-element.189, f32[2048]{0:T(1024)S(1)} %select_maximum_fusion.2, pred[512]{0:T(512)(128)(4,1)S(1)} %dynamic-slice_reduce_fusion.2, f32[2048,128]{1,0:T(8,128)S(1)} %get-tuple-element.205, f32[2048]{0:T(1024)S(1)} %get-tuple-element.191, ...), kind=kOutput, calls=%fused_computation.5.clone.1 | convolution fusion | flops 274464768 | bytes 6439429 | tf_op jit(solution)/shard_map/while/body/eval_jaxpr/dot_general | solution.py:41
  147.2 1.6 fusion.91
  150.2 2.9 %convolution_add_fusion.3 = f32[2048,128]{1,0:T(8,128)S(1)} fusion(f32[512,2048]{1,0:T(8,128)S(1)} %get-tuple-element.189, f32[2048]{0:T(1024)S(1)} %select_maximum_fusion.2, pred[512]{0:T(512)(128)(4,1)S(1)} %dynamic-slice_reduce_fusion.2, f32[2048,128]{1,0:T(8,128)S(1)} %get-tuple-element.205, f32[2048]{0:T(1024)S(1)} %get-tuple-element.191, ...), kind=kOutput, calls=%fused_computation.5.clone.1 | convolution fusion | flops 274464768 | bytes 6439429 | tf_op jit(solution)/shard_map/while/body/eval_jaxpr/dot_general | solution.py:41
  153.2 1.6 fusion.91
  154.9 1.3 fusion.92
  156.2 2.9 %convolution_add_fusion.3 = f32[2048,128]{1,0:T(8,128)S(1)} fusion(f32[512,2048]{1,0:T(8,128)S(1)} %get-tuple-element.189, f32[2048]{0:T(1024)S(1)} %select_maximum_fusion.2, pred[512]{0:T(512)(128)(4,1)S(1)} %dynamic-slice_reduce_fusion.2, f32[2048,128]{1,0:T(8,128)S(1)} %get-tuple-element.205, f32[2048]{0:T(1024)S(1)} %get-tuple-element.191, ...), kind=kOutput, calls=%fused_computation.5.clone.1 | convolution fusion | flops 274464768 | bytes 6439429 | tf_op jit(solution)/shard_map/while/body/eval_jaxpr/dot_general | solution.py:41
  159.2 1.6 fusion.91
  162.1 2.9 %convolution_add_fusion.3 = f32[2048,128]{1,0:T(8,128)S(1)} fusion(f32[512,2048]{1,0:T(8,128)S(1)} %get-tuple-element.189, f32[2048]{0:T(1024)S(1)} %select_maximum_fusion.2, pred[512]{0:T(512)(128)(4,1)S(1)} %dynamic-slice_reduce_fusion.2, f32[2048,128]{1,0:T(8,128)S(1)} %get-tuple-element.205, f32[2048]{0:T(1024)S(1)} %get-tuple-element.191, ...), kind=kOutput, calls=%fused_computation.5.clone.1 | convolution fusion | flops 274464768 | bytes 6439429 | tf_op jit(solution)/shard_map/while/body/eval_jaxpr/dot_general | solution.py:41
  165.1 1.6 fusion.91
  168.1 2.9 %convolution_add_fusion.3 = f32[2048,128]{1,0:T(8,128)S(1)} fusion(f32[512,2048]{1,0:T(8,128)S(1)} %get-tuple-element.189, f32[2048]{0:T(1024)S(1)} %select_maximum_fusion.2, pred[512]{0:T(512)(128)(4,1)S(1)} %dynamic-slice_reduce_fusion.2, f32[2048,128]{1,0:T(8,128)S(1)} %get-tuple-element.205, f32[2048]{0:T(1024)S(1)} %get-tuple-element.191, ...), kind=kOutput, calls=%fused_computation.5.clone.1 | convolution fusion | flops 274464768 | bytes 6439429 | tf_op jit(solution)/shard_map/while/body/eval_jaxpr/dot_general | solution.py:41
  171.1 1.6 fusion.91
  174.1 2.9 %convolution_add_fusion.3 = f32[2048,128]{1,0:T(8,128)S(1)} fusion(f32[512,2048]{1,0:T(8,128)S(1)} %get-tuple-element.189, f32[2048]{0:T(1024)S(1)} %select_maximum_fusion.2, pred[512]{0:T(512)(128)(4,1)S(1)} %dynamic-slice_reduce_fusion.2, f32[2048,128]{1,0:T(8,128)S(1)} %get-tuple-element.205, f32[2048]{0:T(1024)S(1)} %get-tuple-element.191, ...), kind=kOutput, calls=%fused_computation.5.clone.1 | convolution fusion | flops 274464768 | bytes 6439429 | tf_op jit(solution)/shard_map/while/body/eval_jaxpr/dot_general | solution.py:41
  177.1 1.6 fusion.91
  180.0 2.9 %convolution_add_fusion.3 = f32[2048,128]{1,0:T(8,128)S(1)} fusion(f32[512,2048]{1,0:T(8,128)S(1)} %get-tuple-element.189, f32[2048]{0:T(1024)S(1)} %select_maximum_fusion.2, pred[512]{0:T(512)(128)(4,1)S(1)} %dynamic-slice_reduce_fusion.2, f32[2048,128]{1,0:T(8,128)S(1)} %get-tuple-element.205, f32[2048]{0:T(1024)S(1)} %get-tuple-element.191, ...), kind=kOutput, calls=%fused_computation.5.clone.1 | convolution fusion | flops 274464768 | bytes 6439429 | tf_op jit(solution)/shard_map/while/body/eval_jaxpr/dot_general | solution.py:41
  183.0 1.6 fusion.91
  186.0 2.9 %convolution_add_fusion.3 = f32[2048,128]{1,0:T(8,128)S(1)} fusion(f32[512,2048]{1,0:T(8,128)S(1)} %get-tuple-element.189, f32[2048]{0:T(1024)S(1)} %select_maximum_fusion.2, pred[512]{0:T(512)(128)(4,1)S(1)} %dynamic-slice_reduce_fusion.2, f32[2048,128]{1,0:T(8,128)S(1)} %get-tuple-element.205, f32[2048]{0:T(1024)S(1)} %get-tuple-element.191, ...), kind=kOutput, calls=%fused_computation.5.clone.1 | convolution fusion | flops 274464768 | bytes 6439429 | tf_op jit(solution)/shard_map/while/body/eval_jaxpr/dot_general | solution.py:41
  189.0 1.6 fusion.91
  191.9 2.9 %convolution_add_fusion.3 = f32[2048,128]{1,0:T(8,128)S(1)} fusion(f32[512,2048]{1,0:T(8,128)S(1)} %get-tuple-element.189, f32[2048]{0:T(1024)S(1)} %select_maximum_fusion.2, pred[512]{0:T(512)(128)(4,1)S(1)} %dynamic-slice_reduce_fusion.2, f32[2048,128]{1,0:T(8,128)S(1)} %get-tuple-element.205, f32[2048]{0:T(1024)S(1)} %get-tuple-element.191, ...), kind=kOutput, calls=%fused_computation.5.clone.1 | convolution fusion | flops 274464768 | bytes 6439429 | tf_op jit(solution)/shard_map/while/body/eval_jaxpr/dot_general | solution.py:41
  194.9 1.6 fusion.91
  197.9 2.9 %convolution_add_fusion.3 = f32[2048,128]{1,0:T(8,128)S(1)} fusion(f32[512,2048]{1,0:T(8,128)S(1)} %get-tuple-element.189, f32[2048]{0:T(1024)S(1)} %select_maximum_fusion.2, pred[512]{0:T(512)(128)(4,1)S(1)} %dynamic-slice_reduce_fusion.2, f32[2048,128]{1,0:T(8,128)S(1)} %get-tuple-element.205, f32[2048]{0:T(1024)S(1)} %get-tuple-element.191, ...), kind=kOutput, calls=%fused_computation.5.clone.1 | convolution fusion | flops 274464768 | bytes 6439429 | tf_op jit(solution)/shard_map/while/body/eval_jaxpr/dot_general | solution.py:41
  200.9 1.6 fusion.91
  203.9 2.9 %convolution_add_fusion.3 = f32[2048,128]{1,0:T(8,128)S(1)} fusion(f32[512,2048]{1,0:T(8,128)S(1)} %get-tuple-element.189, f32[2048]{0:T(1024)S(1)} %select_maximum_fusion.2, pred[512]{0:T(512)(128)(4,1)S(1)} %dynamic-slice_reduce_fusion.2, f32[2048,128]{1,0:T(8,128)S(1)} %get-tuple-element.205, f32[2048]{0:T(1024)S(1)} %get-tuple-element.191, ...), kind=kOutput, calls=%fused_computation.5.clone.1 | convolution fusion | flops 274464768 | bytes 6439429 | tf_op jit(solution)/shard_map/while/body/eval_jaxpr/dot_general | solution.py:41
  206.9 1.6 fusion.91
  209.8 2.9 %convolution_add_fusion.3 = f32[2048,128]{1,0:T(8,128)S(1)} fusion(f32[512,2048]{1,0:T(8,128)S(1)} %get-tuple-element.189, f32[2048]{0:T(1024)S(1)} %select_maximum_fusion.2, pred[512]{0:T(512)(128)(4,1)S(1)} %dynamic-slice_reduce_fusion.2, f32[2048,128]{1,0:T(8,128)S(1)} %get-tuple-element.205, f32[2048]{0:T(1024)S(1)} %get-tuple-element.191, ...), kind=kOutput, calls=%fused_computation.5.clone.1 | convolution fusion | flops 274464768 | bytes 6439429 | tf_op jit(solution)/shard_map/while/body/eval_jaxpr/dot_general | solution.py:41
  212.8 1.6 fusion.91
  215.8 2.9 %convolution_add_fusion.3 = f32[2048,128]{1,0:T(8,128)S(1)} fusion(f32[512,2048]{1,0:T(8,128)S(1)} %get-tuple-element.189, f32[2048]{0:T(1024)S(1)} %select_maximum_fusion.2, pred[512]{0:T(512)(128)(4,1)S(1)} %dynamic-slice_reduce_fusion.2, f32[2048,128]{1,0:T(8,128)S(1)} %get-tuple-element.205, f32[2048]{0:T(1024)S(1)} %get-tuple-element.191, ...), kind=kOutput, calls=%fused_computation.5.clone.1 | convolution fusion | flops 274464768 | bytes 6439429 | tf_op jit(solution)/shard_map/while/body/eval_jaxpr/dot_general | solution.py:41
  218.9 3.6 %fusion.33 = f32[2048]{0:T(1024)S(1)} fusion(f32[2048,512]{0,1:T(8,128)} %get-tuple-element.134, f32[2048]{0:T(1024)S(1)} %max.6, s32[2048]{0:T(1024)S(1)} %add_select_fusion, pred[512]{0:T(512)(128)(4,1)S(1)} %iota_compare_fusion.2), kind=kLoop, calls=%fused_computation.45 | loop fusion | flops 5240832 | bytes 4219392 | tf_op jit(solution)/shard_map/reduce_sum | solution.py:40
  222.6 7.5 %fusion.37 = bf16[2048,128]{1,0:T(8,128)(2,1)S(1)} fusion(f32[2048,512]{0,1:T(8,128)} %get-tuple-element.134, f32[2048]{0:T(1024)S(1)} %max.6, s32[2048]{0:T(1024)S(1)} %add_select_fusion, pred[512]{0:T(512)(128)(4,1)S(1)} %iota_compare_fusion.2, f32[2048,128]{1,0:T(8,128)S(1)} %get-tuple-element.49, bf16[5120,128]{1,0:T(8,128)(2,1)S(1)} %copy-done, ...), kind=kOutput, calls=%fused_computation.50 | convolution fusion | flops 956366848 | bytes 12376576 | tf_op jit(solution)/shard_map/dot_general | solution.py:41
  231.1 29.7 %all-gather.8.cloned.1.call-done = bf16[512,2048]{0,1:T(8,128)(2,1)} async-done(((bf16[512,512]{0,1:T(8,128)(2,1)}), bf16[512,2048]{0,1:T(8,128)(2,1)}) %all-gather.8.cloned.1.call-update) | async-done | bytes 2097168 | tf_op jit(solution)/shard_map/all_gather | solution.py:133
  260.8 7.1 %fusion.35 = bf16[1,512,1280]{2,1,0:T(8,128)(2,1)} fusion(bf16[512,2048]{0,1:T(8,128)(2,1)} %all-gather.8.cloned.1.call-done, bf16[2048,1280]{1,0:T(8,128)(2,1)} %param.17, pred[512]{0:T(512)(128)(4,1)S(1)} %iota_compare_fusion.2), kind=kOutput, calls=%fused_computation.47 | convolution fusion | flops 2685665280 | bytes 8651264 | tf_op jit(solution)/shard_map/dot_general | solution.py:132
  (112 shorter events, 26.0 us)
Async XLA Ops:
  6.5 216.0 %copy-start = (bf16[5120,128]{1,0:T(8,128)(2,1)S(1)}, bf16[5120,128]{1,0:T(8,128)(2,1)}, u32[]{:S(2)}) copy-start(bf16[5120,128]{1,0:T(8,128)(2,1)} %param.16) | copy-start | bytes 3932164
  6.5 62.5 %all-gather.6.cloned.1.call-start = ((), (), s32[]{:S(2)}) async-start(), calls=%async_computation.1 | async-start | bytes 6553600 | tf_op jit(solution)/shard_map/all_gather | solution.py:77
  7.3 111.2 %all-gather.4.cloned.1.call-start = ((), (), s32[]{:S(2)}) async-start(), calls=%async_computation | async-start | bytes 4325376 | tf_op jit(solution)/shard_map/all_gather | solution.py:111
  8.0 252.8 %all-gather.8.cloned.1.call-start = ((), (), s32[]{:S(2)}) async-start(), calls=%async_computation.2 | async-start | bytes 2621440 | tf_op jit(solution)/shard_map/all_gather | solution.py:133
  21.6 51.2 %copy-start.2 = (f32[5120]{0:T(1024)S(1)}, f32[5120]{0:T(1024)}, u32[]{:S(2)}) copy-start(f32[5120]{0:T(1024)} %param.13) | copy-start | bytes 61444
  69.0 4.0 %copy-start.1 = (bf16[1,512,5120]{2,1,0:T(8,128)(2,1)S(1)}, bf16[1,512,5120]{2,1,0:T(8,128)(2,1)}, u32[]{:S(2)}) copy-start(bf16[1,512,5120]{2,1,0:T(8,128)(2,1)} %all-gather.6.cloned.1.call-done) | copy-start | bytes 15728644
Sparse Core Ops, SparseCore 0:
  9.0 59.9 all-gather.5
  71.2 47.1 all-gather.3
  231.2 29.5 all-gather.7
where the time goes:
time: 275 us; the launch traced here: 274 us
  waiting for transfers between devices  108 us (39%)
  matrix products  102 us (37%)
  other arithmetic  30.1 us (11%)
  local copies, waits for them, and re-layouts  18.2 us (7%)
  between operations  15.3 us (6%)
    dot_general x17, matrix products, online_block(): jnp.dot(weights.astype(jnp.bfloat16), block_values, preferred_element_typ...  54.4 us
    all_gather x1, waiting for transfers between devices, local(): whole = lax.all_gather(hidden_in, 'head', axis=2, tiled=True)  46.2 us
    all_gather x1, waiting for transfers between devices, local(): piece = lax.all_gather(prefix_cache, 'tok', axis=0, tiled=True)  30.4 us
    dot_general x17, matrix products, online_block(): lax.dot_general(queries, block_keys, (((1,), (1,)), ((), ())), preferred_...  29.7 us
    all_gather x1, waiting for transfers between devices, local(): lax.all_gather(pieces, 'head', axis=1, tiled=True)  29.7 us
    reduce_sum x17, other arithmetic, online_block(): total = total * factor + jnp.sum(weights, axis=1)  24 us
    dot_general x1, local copies, waits for them, and re-layouts, local(): jnp.dot(normed, w_query, preferred_element_type=jnp.float32)  7.81 us
    dot_general x1, matrix products, local(): jnp.dot(lax.all_gather(pieces, 'head', axis=1, tiled=True), w_out, prefer...  7.12 us
  transfers between devices with their start and end apart: 3, of which 3 were waited for; matrix products, arithmetic and copies ran while one was open for 11% of the time, Pallas kernels for 0%

commit v1 on v0

--- a/solution.py
+++ b/solution.py
@@ -3,12 +3,26 @@
 import jax.numpy as jnp
 from jax import lax
 from jax.sharding import PartitionSpec as P
+from jax.lax import axis_index, axis_size, ppermute
 
 HD = 128
 PREFIX = 4096
 THETA = 100000000.0
 EPS = 1e-05
 NEG = -1e30
+
+
+def ends_bind(matrix, bus_axis):
+    n_all = axis_size(bus_axis)
+    blocks_here = [(num, (num + 1) % n_all) for num in range(n_all)]
+    all_rows = [(num, (num - 1) % n_all) for num in range(n_all)]
+    res, q_next = ([matrix], [matrix])
+    for _ in range(n_all // 2):
+        res.append(ppermute(res[-1], bus_axis, blocks_here))
+    for _ in [*range((n_all - 1) // 2)]:
+        q_next.append(ppermute(q_next[-1], perm=all_rows, axis_name=bus_axis))
+    clean = jnp.concatenate([*res[::-1], *q_next[1:]], axis=2)
+    return jnp.roll(clean, (axis_index(bus_axis) - n_all // 2) * matrix.shape[2], axis=2)
 
 
 def rope_angles(positions, size):
@@ -74,7 +88,7 @@
     request_group,
 ):
     local_len = hidden_in.shape[1]
-    whole = lax.all_gather(hidden_in, "head", axis=2, tiled=True)
+    whole = ends_bind(hidden_in, "head")
     flat = whole.reshape(local_len, whole.shape[2]).astype(jnp.float32)
     inverse = lax.rsqrt(jnp.mean(flat * flat, axis=1, keepdims=True) + EPS)
     normed = (flat * inverse * norm_gain[None, :]).astype(jnp.bfloat16)

time: 275 us -> 341 us (1.24)
  matrix products: 102 us -> 147 us
  other arithmetic: 30.1 us -> 68 us
  waiting for transfers between devices: 108 us -> 75.8 us
  local copies, waits for them, and re-layouts: 18.2 us -> 27.6 us
  starting transfers between devices: 0.08 us -> 4.9 us
    all_gather x1 -> x0, waiting for transfers between devices: 46.2 us -> none  [local(): whole = lax.all_gather(hidden_in, 'head', axis=2, tiled=True)]
    ppermute x0 -> x3, waiting for transfers between devices: none -> 43.1 us  [the longest x2 43.1 us: ends_bind(): res.append(ppermute(res[-1], bus_axis, blocks_here))]
    reduce_sum x17, other arithmetic: 24 us -> 61.1 us  [online_block(): total = total * factor + jnp.sum(weights, axis=1)]
    dot_general x17, matrix products: 29.7 us -> 61.3 us  [online_block(): lax.dot_general(queries, block_keys, (((1,), (1,)), ((), ())), preferred_...]
    all_gather x1, waiting for transfers between devices: 30.4 us -> 0.01 us  [local(): piece = lax.all_gather(prefix_cache, 'tok', axis=0, tiled=True)]
    dot_general x17, matrix products: 54.4 us -> 69 us  [online_block(): jnp.dot(weights.astype(jnp.bfloat16), block_values, preferred_element_typ...]
    unnamed x6 -> x19, local copies, waits for them, and re-layouts: 0.3 us -> 7.91 us
    ppermute x0 -> x3, starting transfers between devices: none -> 4.86 us  [the longest x1 2.67 us: ends_bind(): q_next.append(ppermute(q_next[-1], perm=all_rows, axis_name=bus_axis))]
  transfers between devices with their start and end apart: 3 -> 5, of which waited for: 3 -> 3; matrix products, arithmetic and copies ran while one was open for 11% -> 12% of each run, Pallas kernels for 0% -> 0%
where the time goes in v1:
time: 341 us; the launch traced here: 340 us
  matrix products  147 us (43%)
  waiting for transfers between devices  75.8 us (22%)
  other arithmetic  68 us (20%)
  local copies, waits for them, and re-layouts  27.6 us (8%)
  between operations  15.6 us (5%)
  starting transfers between devices  4.9 us (1%)
    dot_general x17, matrix products, online_block(): jnp.dot(weights.astype(jnp.bfloat16), block_values, preferred_element_typ...  69 us
    dot_general x17, matrix products, online_block(): lax.dot_general(queries, block_keys, (((1,), (1,)), ((), ())), preferred_...  61.3 us
    reduce_sum x17, other arithmetic, online_block(): total = total * factor + jnp.sum(weights, axis=1)  61.1 us
    ppermute x2, waiting for transfers between devices, ends_bind(): res.append(ppermute(res[-1], bus_axis, blocks_here))  43.1 us
    all_gather x1, waiting for transfers between devices, local(): lax.all_gather(pieces, 'head', axis=1, tiled=True)  32 us
    dot_general x1, local copies, waits for them, and re-layouts, local(): jnp.dot(normed, w_query, preferred_element_type=jnp.float32)  8.09 us
    unnamed x19, local copies, waits for them, and re-layouts  7.91 us
    dot_general x1, matrix products, local(): jnp.dot(lax.all_gather(pieces, 'head', axis=1, tiled=True), w_out, prefer...  7.12 us
  transfers between devices with their start and end apart: 5, of which 3 were waited for; matrix products, arithmetic and copies ran while one was open for 12% of the time, Pallas kernels for 0%

profile of v1, /device:TPU:1, one launch (start us, length us, event | category | flops | bytes accessed | tf_op | source)
XLA Modules:
  0.0 339.6 jit_solution(5467055903908828194)
XLA Ops:
  9.5 30.1 %collective-permute-done = bf16[1,512,1280]{2,1,0:T(8,128)(2,1)} collective-permute-done((bf16[1,512,1280]{2,1,0:T(8,128)(2,1)}, bf16[1,512,1280]{2,1,0:T(8,128)(2,1)}, u32[]{:S(2)}, u32[]{:S(2)}) %collective-permute-start) | collective-permute-done | bytes 1310752 | tf_op jit(solution)/shard_map/ppermute | solution.py:21
  48.2 8.1 %copy.24 = bf16[512,5120]{1,0:T(8,128)(2,1)} copy(bf16[512,5120]{0,1:T(8,128)(2,1)} %bitcast.66) | data formatting | bytes 10485760 | tf_op jit(solution)/shard_map/dot_general | solution.py:104
  57.1 13.0 %collective-permute-done.1 = bf16[1,512,1280]{2,1,0:T(8,128)(2,1)} collective-permute-done((bf16[1,512,1280]{2,1,0:T(8,128)(2,1)}, bf16[1,512,1280]{2,1,0:T(8,128)(2,1)}, u32[]{:S(2)}, u32[]{:S(2)}) %collective-permute-start.1) | collective-permute-done | bytes 1310752 | tf_op jit(solution)/shard_map/ppermute | solution.py:21
  79.7 4.5 %fusion.21 = f32[512]{0:T(512)S(1)} fusion(bf16[1,512,10240]{2,1,0:T(8,128)(2,1)S(1)} %constant_dynamic-update-slice_fusion, s32[]{:T(128)S(6)} %select_n.52), kind=kLoop, calls=%fused_computation.30 | loop fusion | flops 7863808 | bytes 5244932 | tf_op jit(solution)/shard_map/reduce_sum | solution.py:93
  84.3 3.8 %fusion.27 = f32[512,4,128]{0,2,1:T(8,128)S(1)} fusion(bf16[4,128,5120]{2,1,0:T(8,128)(2,1)S(1)} %bitcast.69, f32[5120]{0:T(1024)S(1)} %copy-done.4, f32[512]{0:T(512)S(1)} %add_rsqrt_fusion, bf16[1,512,10240]{2,1,0:T(8,128)(2,1)S(1)} %constant_dynamic-update-slice_fusion, s32[]{:T(128)S(6)} %select_n.52), kind=kOutput, calls=%fused_computation.36 | convolution fusion | flops 2694840320 | bytes 11556868 | tf_op jit(solution)/shard_map/dot_general | solution.py:104
  88.7 6.1 %convolution_bitcast_fusion = f32[512,1,128]{0,2,1:T(8,128)S(1)} fusion(bf16[5120,128]{1,0:T(8,128)(2,1)} %param.15, f32[5120]{0:T(1024)S(1)} %copy-done.4, f32[512]{0:T(512)S(1)} %add_rsqrt_fusion, bf16[1,512,10240]{2,1,0:T(8,128)(2,1)} %copy-done.3, s32[]{:T(128)S(6)} %select_n.52), kind=kOutput, calls=%fused_computation.55 | convolution fusion | flops 681574400 | bytes 6838276 | tf_op jit(solution)/shard_map/dot_general | solution.py:108
  98.7 4.8 %fusion.69 = (bf16[64,1,128,128]{3,2,1,0:T(8,128)(2,1)}, bf16[64,1,128,128]{3,2,1,0:T(8,128)(2,1)}) fusion(bf16[64,2,128,128]{3,2,1,0:T(8,128)(2,1)} %all-gather.3.cloned.1.call-done), kind=kLoop, calls=%fused_computation.104 | loop fusion | bytes 8388608 | tf_op jit(solution)/shard_map/slice | solution.py:132
  103.5 177.1 %while.15 = (s32[]{:T(128)}, f32[2048]{0:T(1024)S(1)}, f32[2048]{0:T(1024)S(1)}, f32[2048,128]{1,0:T(8,128)}, pred[16,1,512]{2,1,0:T(4,128)(4,1)S(1)}, /*index=5...) while((s32[]{:T(128)}, f32[2048]{0:T(1024)S(1)}, ...), condition=%wide.region_5.6_spmd.clone, body=%wide.region_2.5_spmd.clone.sunk | while | flops 551299072 | bytes 32378512 | solution.py:74
  103.5 3.6 %fusion.87 = (f32[2048]{0:T(1024)S(1)}, f32[512,2048]{1,0:T(8,128)}) fusion(pred[512]{0:T(512)(128)(4,1)S(1)} %dynamic-slice_reduce_fusion.2, bf16[2048,128]{1,0:T(8,128)(2,1)S(1)} %get-tuple-element.218, bf16[16,512,128]{2,1,0:T(8,128)(2,1)} %get-tuple-element.217, s32[]{:T(128)} %get-tuple-element.202), kind=kOutput, calls=%fused_computation.2.clone.1 | convolution fusion | flops 271579136 | bytes 4858880 | tf_op jit(solution)/shard_map/while/body/eval_jaxpr/dot_general | solution.py:47
  107.2 3.6 %fusion.88 = f32[2048]{0:T(1024)S(1)} fusion(f32[512,2048]{1,0:T(8,128)} %get-tuple-element.189, f32[2048]{0:T(1024)S(1)} %select_maximum_fusion.2, pred[512]{0:T(512)(128)(4,1)S(1)} %dynamic-slice_reduce_fusion.2), kind=kLoop, calls=%fused_computation.3.clone.1 | loop fusion | flops 5240832 | bytes 4211200 | tf_op jit(solution)/shard_map/while/body/eval_jaxpr/reduce_sum | solution.py:54
  114.2 3.6 %fusion.87 = (f32[2048]{0:T(1024)S(1)}, f32[512,2048]{1,0:T(8,128)}) fusion(pred[512]{0:T(512)(128)(4,1)S(1)} %dynamic-slice_reduce_fusion.2, bf16[2048,128]{1,0:T(8,128)(2,1)S(1)} %get-tuple-element.218, bf16[16,512,128]{2,1,0:T(8,128)(2,1)} %get-tuple-element.217, s32[]{:T(128)} %get-tuple-element.202), kind=kOutput, calls=%fused_computation.2.clone.1 | convolution fusion | flops 271579136 | bytes 4858880 | tf_op jit(solution)/shard_map/while/body/eval_jaxpr/dot_general | solution.py:47
  117.9 3.6 %fusion.88 = f32[2048]{0:T(1024)S(1)} fusion(f32[512,2048]{1,0:T(8,128)} %get-tuple-element.189, f32[2048]{0:T(1024)S(1)} %select_maximum_fusion.2, pred[512]{0:T(512)(128)(4,1)S(1)} %dynamic-slice_reduce_fusion.2), kind=kLoop, calls=%fused_computation.3.clone.1 | loop fusion | flops 5240832 | bytes 4211200 | tf_op jit(solution)/shard_map/while/body/eval_jaxpr/reduce_sum | solution.py:54
  121.5 3.8 %convolution_add_fusion.3 = f32[2048,128]{1,0:T(8,128)} fusion(f32[512,2048]{1,0:T(8,128)S(1)} %copy-done.1, f32[2048]{0:T(1024)S(1)} %select_maximum_fusion.2, pred[512]{0:T(512)(128)(4,1)S(1)} %dynamic-slice_reduce_fusion.2, f32[2048,128]{1,0:T(8,128)} %get-tuple-element.205, f32[2048]{0:T(1024)S(1)} %get-tuple-element.191, pred[]{:T(512)S(6)} %compare.4, ...), kind=kOutput, calls=%fused_computation.5.clone.1 | convolution fusion | flops 274464768 | bytes 6439937 | tf_op jit(solution)/shard_map/while/body/eval_jaxpr/dot_general | solution.py:55
  125.3 3.6 %fusion.87 = (f32[2048]{0:T(1024)S(1)}, f32[512,2048]{1,0:T(8,128)}) fusion(pred[512]{0:T(512)(128)(4,1)S(1)} %dynamic-slice_reduce_fusion.2, bf16[2048,128]{1,0:T(8,128)(2,1)S(1)} %get-tuple-element.218, bf16[16,512,128]{2,1,0:T(8,128)(2,1)} %get-tuple-element.217, s32[]{:T(128)} %get-tuple-element.202), kind=kOutput, calls=%fused_computation.2.clone.1 | convolution fusion | flops 271579136 | bytes 4858880 | tf_op jit(solution)/shard_map/while/body/eval_jaxpr/dot_general | solution.py:47
  129.0 3.6 %fusion.88 = f32[2048]{0:T(1024)S(1)} fusion(f32[512,2048]{1,0:T(8,128)} %get-tuple-element.189, f32[2048]{0:T(1024)S(1)} %select_maximum_fusion.2, pred[512]{0:T(512)(128)(4,1)S(1)} %dynamic-slice_reduce_fusion.2), kind=kLoop, calls=%fused_computation.3.clone.1 | loop fusion | flops 5240832 | bytes 4211200 | tf_op jit(solution)/shard_map/while/body/eval_jaxpr/reduce_sum | solution.py:54
  132.6 3.8 %convolution_add_fusion.3 = f32[2048,128]{1,0:T(8,128)} fusion(f32[512,2048]{1,0:T(8,128)S(1)} %copy-done.1, f32[2048]{0:T(1024)S(1)} %select_maximum_fusion.2, pred[512]{0:T(512)(128)(4,1)S(1)} %dynamic-slice_reduce_fusion.2, f32[2048,128]{1,0:T(8,128)} %get-tuple-element.205, f32[2048]{0:T(1024)S(1)} %get-tuple-element.191, pred[]{:T(512)S(6)} %compare.4, ...), kind=kOutput, calls=%fused_computation.5.clone.1 | convolution fusion | flops 274464768 | bytes 6439937 | tf_op jit(solution)/shard_map/while/body/eval_jaxpr/dot_general | solution.py:55
  136.4 3.6 %fusion.87 = (f32[2048]{0:T(1024)S(1)}, f32[512,2048]{1,0:T(8,128)}) fusion(pred[512]{0:T(512)(128)(4,1)S(1)} %dynamic-slice_reduce_fusion.2, bf16[2048,128]{1,0:T(8,128)(2,1)S(1)} %get-tuple-element.218, bf16[16,512,128]{2,1,0:T(8,128)(2,1)} %get-tuple-element.217, s32[]{:T(128)} %get-tuple-element.202), kind=kOutput, calls=%fused_computation.2.clone.1 | convolution fusion | flops 271579136 | bytes 4858880 | tf_op jit(solution)/shard_map/while/body/eval_jaxpr/dot_general | solution.py:47
  140.0 3.6 %fusion.88 = f32[2048]{0:T(1024)S(1)} fusion(f32[512,2048]{1,0:T(8,128)} %get-tuple-element.189, f32[2048]{0:T(1024)S(1)} %select_maximum_fusion.2, pred[512]{0:T(512)(128)(4,1)S(1)} %dynamic-slice_reduce_fusion.2), kind=kLoop, calls=%fused_computation.3.clone.1 | loop fusion | flops 5240832 | bytes 4211200 | tf_op jit(solution)/shard_map/while/body/eval_jaxpr/reduce_sum | solution.py:54
  143.7 3.8 %convolution_add_fusion.3 = f32[2048,128]{1,0:T(8,128)} fusion(f32[512,2048]{1,0:T(8,128)S(1)} %copy-done.1, f32[2048]{0:T(1024)S(1)} %select_maximum_fusion.2, pred[512]{0:T(512)(128)(4,1)S(1)} %dynamic-slice_reduce_fusion.2, f32[2048,128]{1,0:T(8,128)} %get-tuple-element.205, f32[2048]{0:T(1024)S(1)} %get-tuple-element.191, pred[]{:T(512)S(6)} %compare.4, ...), kind=kOutput, calls=%fused_computation.5.clone.1 | convolution fusion | flops 274464768 | bytes 6439937 | tf_op jit(solution)/shard_map/while/body/eval_jaxpr/dot_general | solution.py:55
  147.5 3.6 %fusion.87 = (f32[2048]{0:T(1024)S(1)}, f32[512,2048]{1,0:T(8,128)}) fusion(pred[512]{0:T(512)(128)(4,1)S(1)} %dynamic-slice_reduce_fusion.2, bf16[2048,128]{1,0:T(8,128)(2,1)S(1)} %get-tuple-element.218, bf16[16,512,128]{2,1,0:T(8,128)(2,1)} %get-tuple-element.217, s32[]{:T(128)} %get-tuple-element.202), kind=kOutput, calls=%fused_computation.2.clone.1 | convolution fusion | flops 271579136 | bytes 4858880 | tf_op jit(solution)/shard_map/while/body/eval_jaxpr/dot_general | solution.py:47
  154.8 3.8 %convolution_add_fusion.3 = f32[2048,128]{1,0:T(8,128)} fusion(f32[512,2048]{1,0:T(8,128)S(1)} %copy-done.1, f32[2048]{0:T(1024)S(1)} %select_maximum_fusion.2, pred[512]{0:T(512)(128)(4,1)S(1)} %dynamic-slice_reduce_fusion.2, f32[2048,128]{1,0:T(8,128)} %get-tuple-element.205, f32[2048]{0:T(1024)S(1)} %get-tuple-element.191, pred[]{:T(512)S(6)} %compare.4, ...), kind=kOutput, calls=%fused_computation.5.clone.1 | convolution fusion | flops 274464768 | bytes 6439937 | tf_op jit(solution)/shard_map/while/body/eval_jaxpr/dot_general | solution.py:55
  158.6 3.6 %fusion.87 = (f32[2048]{0:T(1024)S(1)}, f32[512,2048]{1,0:T(8,128)}) fusion(pred[512]{0:T(512)(128)(4,1)S(1)} %dynamic-slice_reduce_fusion.2, bf16[2048,128]{1,0:T(8,128)(2,1)S(1)} %get-tuple-element.218, bf16[16,512,128]{2,1,0:T(8,128)(2,1)} %get-tuple-element.217, s32[]{:T(128)} %get-tuple-element.202), kind=kOutput, calls=%fused_computation.2.clone.1 | convolution fusion | flops 271579136 | bytes 4858880 | tf_op jit(solution)/shard_map/while/body/eval_jaxpr/dot_general | solution.py:47
  165.8 3.8 %convolution_add_fusion.3 = f32[2048,128]{1,0:T(8,128)} fusion(f32[512,2048]{1,0:T(8,128)S(1)} %copy-done.1, f32[2048]{0:T(1024)S(1)} %select_maximum_fusion.2, pred[512]{0:T(512)(128)(4,1)S(1)} %dynamic-slice_reduce_fusion.2, f32[2048,128]{1,0:T(8,128)} %get-tuple-element.205, f32[2048]{0:T(1024)S(1)} %get-tuple-element.191, pred[]{:T(512)S(6)} %compare.4, ...), kind=kOutput, calls=%fused_computation.5.clone.1 | convolution fusion | flops 274464768 | bytes 6439937 | tf_op jit(solution)/shard_map/while/body/eval_jaxpr/dot_general | solution.py:55
  169.7 3.6 %fusion.87 = (f32[2048]{0:T(1024)S(1)}, f32[512,2048]{1,0:T(8,128)}) fusion(pred[512]{0:T(512)(128)(4,1)S(1)} %dynamic-slice_reduce_fusion.2, bf16[2048,128]{1,0:T(8,128)(2,1)S(1)} %get-tuple-element.218, bf16[16,512,128]{2,1,0:T(8,128)(2,1)} %get-tuple-element.217, s32[]{:T(128)} %get-tuple-element.202), kind=kOutput, calls=%fused_computation.2.clone.1 | convolution fusion | flops 271579136 | bytes 4858880 | tf_op jit(solution)/shard_map/while/body/eval_jaxpr/dot_general | solution.py:47
  173.3 3.6 %fusion.88 = f32[2048]{0:T(1024)S(1)} fusion(f32[512,2048]{1,0:T(8,128)} %get-tuple-element.189, f32[2048]{0:T(1024)S(1)} %select_maximum_fusion.2, pred[512]{0:T(512)(128)(4,1)S(1)} %dynamic-slice_reduce_fusion.2), kind=kLoop, calls=%fused_computation.3.clone.1 | loop fusion | flops 5240832 | bytes 4211200 | tf_op jit(solution)/shard_map/while/body/eval_jaxpr/reduce_sum | solution.py:54
  176.9 3.8 %convolution_add_fusion.3 = f32[2048,128]{1,0:T(8,128)} fusion(f32[512,2048]{1,0:T(8,128)S(1)} %copy-done.1, f32[2048]{0:T(1024)S(1)} %select_maximum_fusion.2, pred[512]{0:T(512)(128)(4,1)S(1)} %dynamic-slice_reduce_fusion.2, f32[2048,128]{1,0:T(8,128)} %get-tuple-element.205, f32[2048]{0:T(1024)S(1)} %get-tuple-element.191, pred[]{:T(512)S(6)} %compare.4, ...), kind=kOutput, calls=%fused_computation.5.clone.1 | convolution fusion | flops 274464768 | bytes 6439937 | tf_op jit(solution)/shard_map/while/body/eval_jaxpr/dot_general | solution.py:55
  180.8 3.6 %fusion.87 = (f32[2048]{0:T(1024)S(1)}, f32[512,2048]{1,0:T(8,128)}) fusion(pred[512]{0:T(512)(128)(4,1)S(1)} %dynamic-slice_reduce_fusion.2, bf16[2048,128]{1,0:T(8,128)(2,1)S(1)} %get-tuple-element.218, bf16[16,512,128]{2,1,0:T(8,128)(2,1)} %get-tuple-element.217, s32[]{:T(128)} %get-tuple-element.202), kind=kOutput, calls=%fused_computation.2.clone.1 | convolution fusion | flops 271579136 | bytes 4858880 | tf_op jit(solution)/shard_map/while/body/eval_jaxpr/dot_general | solution.py:47
  188.0 3.8 %convolution_add_fusion.3 = f32[2048,128]{1,0:T(8,128)} fusion(f32[512,2048]{1,0:T(8,128)S(1)} %copy-done.1, f32[2048]{0:T(1024)S(1)} %select_maximum_fusion.2, pred[512]{0:T(512)(128)(4,1)S(1)} %dynamic-slice_reduce_fusion.2, f32[2048,128]{1,0:T(8,128)} %get-tuple-element.205, f32[2048]{0:T(1024)S(1)} %get-tuple-element.191, pred[]{:T(512)S(6)} %compare.4, ...), kind=kOutput, calls=%fused_computation.5.clone.1 | convolution fusion | flops 274464768 | bytes 6439937 | tf_op jit(solution)/shard_map/while/body/eval_jaxpr/dot_general | solution.py:55
  191.9 3.6 %fusion.87 = (f32[2048]{0:T(1024)S(1)}, f32[512,2048]{1,0:T(8,128)}) fusion(pred[512]{0:T(512)(128)(4,1)S(1)} %dynamic-slice_reduce_fusion.2, bf16[2048,128]{1,0:T(8,128)(2,1)S(1)} %get-tuple-element.218, bf16[16,512,128]{2,1,0:T(8,128)(2,1)} %get-tuple-element.217, s32[]{:T(128)} %get-tuple-element.202), kind=kOutput, calls=%fused_computation.2.clone.1 | convolution fusion | flops 271579136 | bytes 4858880 | tf_op jit(solution)/shard_map/while/body/eval_jaxpr/dot_general | solution.py:47
  199.1 3.8 %convolution_add_fusion.3 = f32[2048,128]{1,0:T(8,128)} fusion(f32[512,2048]{1,0:T(8,128)S(1)} %copy-done.1, f32[2048]{0:T(1024)S(1)} %select_maximum_fusion.2, pred[512]{0:T(512)(128)(4,1)S(1)} %dynamic-slice_reduce_fusion.2, f32[2048,128]{1,0:T(8,128)} %get-tuple-element.205, f32[2048]{0:T(1024)S(1)} %get-tuple-element.191, pred[]{:T(512)S(6)} %compare.4, ...), kind=kOutput, calls=%fused_computation.5.clone.1 | convolution fusion | flops 274464768 | bytes 6439937 | tf_op jit(solution)/shard_map/while/body/eval_jaxpr/dot_general | solution.py:55
  203.0 3.6 %fusion.87 = (f32[2048]{0:T(1024)S(1)}, f32[512,2048]{1,0:T(8,128)}) fusion(pred[512]{0:T(512)(128)(4,1)S(1)} %dynamic-slice_reduce_fusion.2, bf16[2048,128]{1,0:T(8,128)(2,1)S(1)} %get-tuple-element.218, bf16[16,512,128]{2,1,0:T(8,128)(2,1)} %get-tuple-element.217, s32[]{:T(128)} %get-tuple-element.202), kind=kOutput, calls=%fused_computation.2.clone.1 | convolution fusion | flops 271579136 | bytes 4858880 | tf_op jit(solution)/shard_map/while/body/eval_jaxpr/dot_general | solution.py:47
  206.6 3.6 %fusion.88 = f32[2048]{0:T(1024)S(1)} fusion(f32[512,2048]{1,0:T(8,128)} %get-tuple-element.189, f32[2048]{0:T(1024)S(1)} %select_maximum_fusion.2, pred[512]{0:T(512)(128)(4,1)S(1)} %dynamic-slice_reduce_fusion.2), kind=kLoop, calls=%fused_computation.3.clone.1 | loop fusion | flops 5240832 | bytes 4211200 | tf_op jit(solution)/shard_map/while/body/eval_jaxpr/reduce_sum | solution.py:54
  210.2 3.8 %convolution_add_fusion.3 = f32[2048,128]{1,0:T(8,128)} fusion(f32[512,2048]{1,0:T(8,128)S(1)} %copy-done.1, f32[2048]{0:T(1024)S(1)} %select_maximum_fusion.2, pred[512]{0:T(512)(128)(4,1)S(1)} %dynamic-slice_reduce_fusion.2, f32[2048,128]{1,0:T(8,128)} %get-tuple-element.205, f32[2048]{0:T(1024)S(1)} %get-tuple-element.191, pred[]{:T(512)S(6)} %compare.4, ...), kind=kOutput, calls=%fused_computation.5.clone.1 | convolution fusion | flops 274464768 | bytes 6439937 | tf_op jit(solution)/shard_map/while/body/eval_jaxpr/dot_general | solution.py:55
  214.0 3.6 %fusion.87 = (f32[2048]{0:T(1024)S(1)}, f32[512,2048]{1,0:T(8,128)}) fusion(pred[512]{0:T(512)(128)(4,1)S(1)} %dynamic-slice_reduce_fusion.2, bf16[2048,128]{1,0:T(8,128)(2,1)S(1)} %get-tuple-element.218, bf16[16,512,128]{2,1,0:T(8,128)(2,1)} %get-tuple-element.217, s32[]{:T(128)} %get-tuple-element.202), kind=kOutput, calls=%fused_computation.2.clone.1 | convolution fusion | flops 271579136 | bytes 4858880 | tf_op jit(solution)/shard_map/while/body/eval_jaxpr/dot_general | solution.py:47
  221.3 3.8 %convolution_add_fusion.3 = f32[2048,128]{1,0:T(8,128)} fusion(f32[512,2048]{1,0:T(8,128)S(1)} %copy-done.1, f32[2048]{0:T(1024)S(1)} %select_maximum_fusion.2, pred[512]{0:T(512)(128)(4,1)S(1)} %dynamic-slice_reduce_fusion.2, f32[2048,128]{1,0:T(8,128)} %get-tuple-element.205, f32[2048]{0:T(1024)S(1)} %get-tuple-element.191, pred[]{:T(512)S(6)} %compare.4, ...), kind=kOutput, calls=%fused_computation.5.clone.1 | convolution fusion | flops 274464768 | bytes 6439937 | tf_op jit(solution)/shard_map/while/body/eval_jaxpr/dot_general | solution.py:55
  225.1 3.6 %fusion.87 = (f32[2048]{0:T(1024)S(1)}, f32[512,2048]{1,0:T(8,128)}) fusion(pred[512]{0:T(512)(128)(4,1)S(1)} %dynamic-slice_reduce_fusion.2, bf16[2048,128]{1,0:T(8,128)(2,1)S(1)} %get-tuple-element.218, bf16[16,512,128]{2,1,0:T(8,128)(2,1)} %get-tuple-element.217, s32[]{:T(128)} %get-tuple-element.202), kind=kOutput, calls=%fused_computation.2.clone.1 | convolution fusion | flops 271579136 | bytes 4858880 | tf_op jit(solution)/shard_map/while/body/eval_jaxpr/dot_general | solution.py:47
  232.4 3.8 %convolution_add_fusion.3 = f32[2048,128]{1,0:T(8,128)} fusion(f32[512,2048]{1,0:T(8,128)S(1)} %copy-done.1, f32[2048]{0:T(1024)S(1)} %select_maximum_fusion.2, pred[512]{0:T(512)(128)(4,1)S(1)} %dynamic-slice_reduce_fusion.2, f32[2048,128]{1,0:T(8,128)} %get-tuple-element.205, f32[2048]{0:T(1024)S(1)} %get-tuple-element.191, pred[]{:T(512)S(6)} %compare.4, ...), kind=kOutput, calls=%fused_computation.5.clone.1 | convolution fusion | flops 274464768 | bytes 6439937 | tf_op jit(solution)/shard_map/while/body/eval_jaxpr/dot_general | solution.py:55
  236.2 3.6 %fusion.87 = (f32[2048]{0:T(1024)S(1)}, f32[512,2048]{1,0:T(8,128)}) fusion(pred[512]{0:T(512)(128)(4,1)S(1)} %dynamic-slice_reduce_fusion.2, bf16[2048,128]{1,0:T(8,128)(2,1)S(1)} %get-tuple-element.218, bf16[16,512,128]{2,1,0:T(8,128)(2,1)} %get-tuple-element.217, s32[]{:T(128)} %get-tuple-element.202), kind=kOutput, calls=%fused_computation.2.clone.1 | convolution fusion | flops 271579136 | bytes 4858880 | tf_op jit(solution)/shard_map/while/body/eval_jaxpr/dot_general | solution.py:47
  243.5 3.8 %convolution_add_fusion.3 = f32[2048,128]{1,0:T(8,128)} fusion(f32[512,2048]{1,0:T(8,128)S(1)} %copy-done.1, f32[2048]{0:T(1024)S(1)} %select_maximum_fusion.2, pred[512]{0:T(512)(128)(4,1)S(1)} %dynamic-slice_reduce_fusion.2, f32[2048,128]{1,0:T(8,128)} %get-tuple-element.205, f32[2048]{0:T(1024)S(1)} %get-tuple-element.191, pred[]{:T(512)S(6)} %compare.4, ...), kind=kOutput, calls=%fused_computation.5.clone.1 | convolution fusion | flops 274464768 | bytes 6439937 | tf_op jit(solution)/shard_map/while/body/eval_jaxpr/dot_general | solution.py:55
  247.3 3.6 %fusion.87 = (f32[2048]{0:T(1024)S(1)}, f32[512,2048]{1,0:T(8,128)}) fusion(pred[512]{0:T(512)(128)(4,1)S(1)} %dynamic-slice_reduce_fusion.2, bf16[2048,128]{1,0:T(8,128)(2,1)S(1)} %get-tuple-element.218, bf16[16,512,128]{2,1,0:T(8,128)(2,1)} %get-tuple-element.217, s32[]{:T(128)} %get-tuple-element.202), kind=kOutput, calls=%fused_computation.2.clone.1 | convolution fusion | flops 271579136 | bytes 4858880 | tf_op jit(solution)/shard_map/while/body/eval_jaxpr/dot_general | solution.py:47
  254.6 3.8 %convolution_add_fusion.3 = f32[2048,128]{1,0:T(8,128)} fusion(f32[512,2048]{1,0:T(8,128)S(1)} %copy-done.1, f32[2048]{0:T(1024)S(1)} %select_maximum_fusion.2, pred[512]{0:T(512)(128)(4,1)S(1)} %dynamic-slice_reduce_fusion.2, f32[2048,128]{1,0:T(8,128)} %get-tuple-element.205, f32[2048]{0:T(1024)S(1)} %get-tuple-element.191, pred[]{:T(512)S(6)} %compare.4, ...), kind=kOutput, calls=%fused_computation.5.clone.1 | convolution fusion | flops 274464768 | bytes 6439937 | tf_op jit(solution)/shard_map/while/body/eval_jaxpr/dot_general | solution.py:55
  258.4 3.6 %fusion.87 = (f32[2048]{0:T(1024)S(1)}, f32[512,2048]{1,0:T(8,128)}) fusion(pred[512]{0:T(512)(128)(4,1)S(1)} %dynamic-slice_reduce_fusion.2, bf16[2048,128]{1,0:T(8,128)(2,1)S(1)} %get-tuple-element.218, bf16[16,512,128]{2,1,0:T(8,128)(2,1)} %get-tuple-element.217, s32[]{:T(128)} %get-tuple-element.202), kind=kOutput, calls=%fused_computation.2.clone.1 | convolution fusion | flops 271579136 | bytes 4858880 | tf_op jit(solution)/shard_map/while/body/eval_jaxpr/dot_general | solution.py:47
  265.7 3.8 %convolution_add_fusion.3 = f32[2048,128]{1,0:T(8,128)} fusion(f32[512,2048]{1,0:T(8,128)S(1)} %copy-done.1, f32[2048]{0:T(1024)S(1)} %select_maximum_fusion.2, pred[512]{0:T(512)(128)(4,1)S(1)} %dynamic-slice_reduce_fusion.2, f32[2048,128]{1,0:T(8,128)} %get-tuple-element.205, f32[2048]{0:T(1024)S(1)} %get-tuple-element.191, pred[]{:T(512)S(6)} %compare.4, ...), kind=kOutput, calls=%fused_computation.5.clone.1 | convolution fusion | flops 274464768 | bytes 6439937 | tf_op jit(solution)/shard_map/while/body/eval_jaxpr/dot_general | solution.py:55
  269.5 3.6 %fusion.87 = (f32[2048]{0:T(1024)S(1)}, f32[512,2048]{1,0:T(8,128)}) fusion(pred[512]{0:T(512)(128)(4,1)S(1)} %dynamic-slice_reduce_fusion.2, bf16[2048,128]{1,0:T(8,128)(2,1)S(1)} %get-tuple-element.218, bf16[16,512,128]{2,1,0:T(8,128)(2,1)} %get-tuple-element.217, s32[]{:T(128)} %get-tuple-element.202), kind=kOutput, calls=%fused_computation.2.clone.1 | convolution fusion | flops 271579136 | bytes 4858880 | tf_op jit(solution)/shard_map/while/body/eval_jaxpr/dot_general | solution.py:47
  276.8 3.8 %convolution_add_fusion.3 = f32[2048,128]{1,0:T(8,128)} fusion(f32[512,2048]{1,0:T(8,128)S(1)} %copy-done.1, f32[2048]{0:T(1024)S(1)} %select_maximum_fusion.2, pred[512]{0:T(512)(128)(4,1)S(1)} %dynamic-slice_reduce_fusion.2, f32[2048,128]{1,0:T(8,128)} %get-tuple-element.205, f32[2048]{0:T(1024)S(1)} %get-tuple-element.191, pred[]{:T(512)S(6)} %compare.4, ...), kind=kOutput, calls=%fused_computation.5.clone.1 | convolution fusion | flops 274464768 | bytes 6439937 | tf_op jit(solution)/shard_map/while/body/eval_jaxpr/dot_general | solution.py:55
  284.2 8.5 %fusion.38 = bf16[2048,128]{1,0:T(8,128)(2,1)S(1)} fusion(f32[2048,512]{0,1:T(8,128)} %get-tuple-element.134, f32[2048]{0:T(1024)S(1)} %max.6, s32[2048]{0:T(1024)S(1)} %add_select_fusion, pred[512]{0:T(512)(128)(4,1)S(1)} %iota_compare_fusion.2, f32[2048,128]{1,0:T(8,128)} %get-tuple-element.49, f32[2048]{0:T(1024)S(1)} %get-tuple-element.121, ...), kind=kOutput, calls=%fused_computation.51 | convolution fusion | flops 956366848 | bytes 12376580 | tf_op jit(solution)/shard_map/dot_general | solution.py:55
  293.7 32.0 %all-gather.5.cloned.1.call-done = bf16[512,2048]{0,1:T(8,128)(2,1)} async-done(((bf16[512,512]{0,1:T(8,128)(2,1)}), bf16[512,2048]{0,1:T(8,128)(2,1)}) %all-gather.5.cloned.1.call-update) | async-done | bytes 2097168 | tf_op jit(solution)/shard_map/all_gather | solution.py:147
  325.7 7.1 %fusion.36 = bf16[1,512,1280]{2,1,0:T(8,128)(2,1)} fusion(bf16[512,2048]{0,1:T(8,128)(2,1)} %all-gather.5.cloned.1.call-done, bf16[2048,1280]{1,0:T(8,128)(2,1)} %param.17, pred[512]{0:T(512)(128)(4,1)S(1)} %iota_compare_fusion.2), kind=kOutput, calls=%fused_computation.48 | convolution fusion | flops 2685665280 | bytes 8651264 | tf_op jit(solution)/shard_map/dot_general | solution.py:146
  (162 shorter events, 69.0 us)
Async XLA Ops:
  6.5 277.6 %copy-start = (bf16[5120,128]{1,0:T(8,128)(2,1)S(1)}, bf16[5120,128]{1,0:T(8,128)(2,1)}, u32[]{:S(2)}) copy-start(bf16[5120,128]{1,0:T(8,128)(2,1)} %param.16) | copy-start | bytes 3932164
  6.5 92.2 %all-gather.3.cloned.1.call-start = ((), (), s32[]{:S(2)}) async-start(), calls=%async_computation | async-start | bytes 4325376 | tf_op jit(solution)/shard_map/all_gather | solution.py:125
  7.3 318.4 %all-gather.5.cloned.1.call-start = ((), (), s32[]{:S(2)}) async-start(), calls=%async_computation.1 | async-start | bytes 2621440 | tf_op jit(solution)/shard_map/all_gather | solution.py:147
  7.3 32.3 %collective-permute-start = (bf16[1,512,1280]{2,1,0:T(8,128)(2,1)}, bf16[1,512,1280]{2,1,0:T(8,128)(2,1)}, u32[]{:S(2)}, u32[]{:S(2)}) collective-permute-start(bf16[1,512,1280]{2,1,0:T(8,128)(2,1)} %param.12), channel_id=1, source_target_pairs={{0,1},{1,2},{2,3},{3,0},{4,5},{5,6},{6,7},{7,4},{8,9},{9,10},{10,1... | collective-permute-start | bytes 3932168 | tf_op jit(solution)/shard_map/ppermute | solution.py:21
  39.6 30.5 %collective-permute-start.1 = (bf16[1,512,1280]{2,1,0:T(8,128)(2,1)}, bf16[1,512,1280]{2,1,0:T(8,128)(2,1)}, u32[]{:S(2)}, u32[]{:S(2)}) collective-permute-start(bf16[1,512,1280]{2,1,0:T(8,128)(2,1)} %collective-permute-done), channel_id=1, source_target_pairs={{0,1},{1,2},{2,3},{3,0},{4,5},{5,6},{6,7},{7,4},{8,9},{9,10},{10,1... | collective-permute-start | bytes 3932168 | tf_op jit(solution)/shard_map/ppermute | solution.py:21
  39.6 33.7 %collective-permute-start.2 = (bf16[1,512,1280]{2,1,0:T(8,128)(2,1)}, bf16[1,512,1280]{2,1,0:T(8,128)(2,1)}, u32[]{:S(2)}, u32[]{:S(2)}) collective-permute-start(bf16[1,512,1280]{2,1,0:T(8,128)(2,1)} %param.12), channel_id=1, source_target_pairs={{0,3},{1,0},{2,1},{3,2},{4,7},{5,4},{6,5},{7,6},{8,11},{9,8},{10,9... | collective-permute-start | bytes 3932168 | tf_op jit(solution)/shard_map/ppermute | solution.py:23
  56.3 16.8 %copy-start.2 = (bf16[1,512,1280]{2,1,0:T(8,128)(2,1)S(1)}, bf16[1,512,1280]{2,1,0:T(8,128)(2,1)}, u32[]{:S(2)}) copy-start(bf16[1,512,1280]{2,1,0:T(8,128)(2,1)} %param.12) | copy-start | bytes 3932164
  76.3 8.0 %slice-start = ((s8[5242880]{0:T(1024)(128)(4,1)}), s8[4194304]{0:T(1024)(128)(4,1)S(1)}, s32[]{:S(2)}) async-start(s8[5242880]{0:T(1024)(128)(4,1)} %bitcast.67), calls=%async_computation.2 | async-start | bytes 8388608
  78.1 6.2 %slice-start.1 = ((s8[5242880]{0:T(1024)(128)(4,1)}), s8[1048576]{0:T(1024)(128)(4,1)S(1)}, s32[]{:S(2)}) async-start(s8[5242880]{0:T(1024)(128)(4,1)} %bitcast.67), calls=%async_computation.3 | async-start | bytes 2097152
  78.1 6.2 %copy-start.4 = (f32[5120]{0:T(1024)S(1)}, f32[5120]{0:T(1024)}, u32[]{:S(2)}) copy-start(f32[5120]{0:T(1024)} %param.13) | copy-start | bytes 61444
  79.7 8.4 %copy-start.3 = (bf16[1,512,10240]{2,1,0:T(8,128)(2,1)}, bf16[1,512,10240]{2,1,0:T(8,128)(2,1)S(1)}, u32[]{:S(2)}) copy-start(bf16[1,512,10240]{2,1,0:T(8,128)(2,1)S(1)} %constant_dynamic-update-slice_fusion) | copy-start | bytes 31457284
  107.2 3.6 %copy-start.1 = (f32[512,2048]{1,0:T(8,128)S(1)}, f32[512,2048]{1,0:T(8,128)}, u32[]{:S(2)}) copy-start(f32[512,2048]{1,0:T(8,128)} %get-tuple-element.189) | copy-start | bytes 12582916 | tf_op jit(solution)/shard_map/while
  117.9 3.6 %copy-start.1 = (f32[512,2048]{1,0:T(8,128)S(1)}, f32[512,2048]{1,0:T(8,128)}, u32[]{:S(2)}) copy-start(f32[512,2048]{1,0:T(8,128)} %get-tuple-element.189) | copy-start | bytes 12582916 | tf_op jit(solution)/shard_map/while
  128.9 3.6 %copy-start.1 = (f32[512,2048]{1,0:T(8,128)S(1)}, f32[512,2048]{1,0:T(8,128)}, u32[]{:S(2)}) copy-start(f32[512,2048]{1,0:T(8,128)} %get-tuple-element.189) | copy-start | bytes 12582916 | tf_op jit(solution)/shard_map/while
  140.0 3.6 %copy-start.1 = (f32[512,2048]{1,0:T(8,128)S(1)}, f32[512,2048]{1,0:T(8,128)}, u32[]{:S(2)}) copy-start(f32[512,2048]{1,0:T(8,128)} %get-tuple-element.189) | copy-start | bytes 12582916 | tf_op jit(solution)/shard_map/while
  151.1 3.6 %copy-start.1 = (f32[512,2048]{1,0:T(8,128)S(1)}, f32[512,2048]{1,0:T(8,128)}, u32[]{:S(2)}) copy-start(f32[512,2048]{1,0:T(8,128)} %get-tuple-element.189) | copy-start | bytes 12582916 | tf_op jit(solution)/shard_map/while
  162.2 3.6 %copy-start.1 = (f32[512,2048]{1,0:T(8,128)S(1)}, f32[512,2048]{1,0:T(8,128)}, u32[]{:S(2)}) copy-start(f32[512,2048]{1,0:T(8,128)} %get-tuple-element.189) | copy-start | bytes 12582916 | tf_op jit(solution)/shard_map/while
  173.3 3.6 %copy-start.1 = (f32[512,2048]{1,0:T(8,128)S(1)}, f32[512,2048]{1,0:T(8,128)}, u32[]{:S(2)}) copy-start(f32[512,2048]{1,0:T(8,128)} %get-tuple-element.189) | copy-start | bytes 12582916 | tf_op jit(solution)/shard_map/while
  184.4 3.6 %copy-start.1 = (f32[512,2048]{1,0:T(8,128)S(1)}, f32[512,2048]{1,0:T(8,128)}, u32[]{:S(2)}) copy-start(f32[512,2048]{1,0:T(8,128)} %get-tuple-element.189) | copy-start | bytes 12582916 | tf_op jit(solution)/shard_map/while
  195.5 3.6 %copy-start.1 = (f32[512,2048]{1,0:T(8,128)S(1)}, f32[512,2048]{1,0:T(8,128)}, u32[]{:S(2)}) copy-start(f32[512,2048]{1,0:T(8,128)} %get-tuple-element.189) | copy-start | bytes 12582916 | tf_op jit(solution)/shard_map/while
  206.6 3.6 %copy-start.1 = (f32[512,2048]{1,0:T(8,128)S(1)}, f32[512,2048]{1,0:T(8,128)}, u32[]{:S(2)}) copy-start(f32[512,2048]{1,0:T(8,128)} %get-tuple-element.189) | copy-start | bytes 12582916 | tf_op jit(solution)/shard_map/while
  217.7 3.6 %copy-start.1 = (f32[512,2048]{1,0:T(8,128)S(1)}, f32[512,2048]{1,0:T(8,128)}, u32[]{:S(2)}) copy-start(f32[512,2048]{1,0:T(8,128)} %get-tuple-element.189) | copy-start | bytes 12582916 | tf_op jit(solution)/shard_map/while
  228.8 3.6 %copy-start.1 = (f32[512,2048]{1,0:T(8,128)S(1)}, f32[512,2048]{1,0:T(8,128)}, u32[]{:S(2)}) copy-start(f32[512,2048]{1,0:T(8,128)} %get-tuple-element.189) | copy-start | bytes 12582916 | tf_op jit(solution)/shard_map/while
  239.8 3.6 %copy-start.1 = (f32[512,2048]{1,0:T(8,128)S(1)}, f32[512,2048]{1,0:T(8,128)}, u32[]{:S(2)}) copy-start(f32[512,2048]{1,0:T(8,128)} %get-tuple-element.189) | copy-start | bytes 12582916 | tf_op jit(solution)/shard_map/while
  250.9 3.6 %copy-start.1 = (f32[512,2048]{1,0:T(8,128)S(1)}, f32[512,2048]{1,0:T(8,128)}, u32[]{:S(2)}) copy-start(f32[512,2048]{1,0:T(8,128)} %get-tuple-element.189) | copy-start | bytes 12582916 | tf_op jit(solution)/shard_map/while
  262.0 3.6 %copy-start.1 = (f32[512,2048]{1,0:T(8,128)S(1)}, f32[512,2048]{1,0:T(8,128)}, u32[]{:S(2)}) copy-start(f32[512,2048]{1,0:T(8,128)} %get-tuple-element.189) | copy-start | bytes 12582916 | tf_op jit(solution)/shard_map/while
  273.1 3.6 %copy-start.1 = (f32[512,2048]{1,0:T(8,128)S(1)}, f32[512,2048]{1,0:T(8,128)}, u32[]{:S(2)}) copy-start(f32[512,2048]{1,0:T(8,128)} %get-tuple-element.189) | copy-start | bytes 12582916 | tf_op jit(solution)/shard_map/while
Sparse Core Ops, SparseCore 0:
  9.6 49.7 all-gather.2
  293.8 31.7 all-gather.4
